TPU v7x, 256 devices: a whole 4x4x8 slice. The times are simulated.
256 devices in a mesh: expert: 16 (over z, core), fsdp: 16 (over x, y).
Axes of the slice: x: 4, y: 4, z: 8, core: 2. Of those that a mesh axis runs over, the one named last changes fastest.
Arguments:
- tokens: bfloat16 [32768, 2048], P(('expert', 'fsdp')), may hold values from -6 to 6
- expert_ids: int32 [32768, 4], P(('expert', 'fsdp')), may hold values from 0 to 15, all different within a row; in each aligned block of 128 rows (0 to 127, 128 to 255, ...) at most 36 rows name the same one
- route_probs: float32 [32768, 4], P(('expert', 'fsdp')), may hold values from 0.1 to 1
- gate_weight: bfloat16 [16, 2048, 704], P('expert', 'fsdp'), may hold values from -0.125 to 0.125
- up_weight: bfloat16 [16, 2048, 704], P('expert', 'fsdp'), may hold values from -0.125 to 0.125
- down_weight: bfloat16 [16, 704, 2048], P('expert', None, 'fsdp'), may hold values from -0.21875 to 0.21875
- cotangent: bfloat16 [32768, 2048], P(('expert', 'fsdp')), may hold values from -0.59765625 to 0.59765625
Outputs:
- mixed: bfloat16 [32768, 2048], P(('expert', 'fsdp'))
- grad_probs: float32 [32768, 4], P(('expert', 'fsdp'))
- grad_tokens: bfloat16 [32768, 2048], P(('expert', 'fsdp'))
- grad_gate: bfloat16 [16, 2048, 704], P('expert', 'fsdp')
- grad_up: bfloat16 [16, 2048, 704], P('expert', 'fsdp')
- grad_down: bfloat16 [16, 704, 2048], P('expert', None, 'fsdp')
Inputs may be any that keep to these rules, and one draw needn't show every extreme that they name: `expert_ids`: each token names 4 different experts; among the 128 tokens of one device no expert is named more than 36 times.
All inputs are finite; a program needn't handle non-finite values.
Results may differ from a plain program's by a relative error of at most 0.014.
Values may be sent and summed in bfloat16 or wider, within the bound.
No kernel may reach another device: no remote copies, remote signals or barrier semaphores. Data moves between devices by JAX's collectives and lax.ppermute only.
A program may use at most 128 MiB of HBM per device.

v0:
```python
import jax
import jax.numpy as jnp
from jax import lax
from jax.sharding import PartitionSpec as P


def routing(id_rows, experts, capacity):
    flat_ids = id_rows.reshape(-1)
    onehot = (flat_ids[:, None] == jnp.arange(experts, dtype=jnp.int32)[None, :]).astype(jnp.int32)
    before = jnp.cumsum(onehot, axis=0) - onehot
    slot_index = jnp.sum(before * onehot, axis=1)
    target = flat_ids * capacity + slot_index
    slots = experts * capacity
    dispatch = jnp.arange(slots, dtype=jnp.int32)[:, None] == target[None, :]
    return (dispatch, jnp.sum(onehot, axis=0))


def expert_forward(routed, live_mask, w_gate, w_up, w_down_blocks):
    gate_pre = jnp.dot(routed, w_gate, preferred_element_type=jnp.float32)
    up_pre = jnp.dot(routed, w_up, preferred_element_type=jnp.float32)
    hidden = (jax.nn.silu(gate_pre) * up_pre * live_mask[:, None]).astype(jnp.bfloat16)
    expert_out = jnp.einsum(
        "sf,jfd->sjd", hidden, w_down_blocks, preferred_element_type=jnp.float32
    ).astype(jnp.bfloat16)
    return (gate_pre, up_pre, hidden, expert_out.reshape(hidden.shape[0], -1))


def expert_backward(routed, grad_rows, gate_pre, up_pre, hidden, w_gate, w_up, w_down_blocks):
    grad_blocks = grad_rows.reshape(grad_rows.shape[0], w_down_blocks.shape[0], -1)
    grad_hidden = jnp.einsum(
        "sjd,jfd->sf", grad_blocks, w_down_blocks, preferred_element_type=jnp.float32
    )
    logistic = jax.nn.sigmoid(gate_pre)
    activated = gate_pre * logistic
    slope = logistic * (1.0 + gate_pre * (1.0 - logistic))
    grad_gate_pre = (grad_hidden * up_pre * slope).astype(jnp.bfloat16)
    grad_up_pre = (grad_hidden * activated).astype(jnp.bfloat16)
    row_grad = (
        jnp.dot(grad_gate_pre, w_gate.T, preferred_element_type=jnp.float32)
        + jnp.dot(grad_up_pre, w_up.T, preferred_element_type=jnp.float32)
    ).astype(jnp.bfloat16)
    term_gate = jnp.dot(routed.T, grad_gate_pre, preferred_element_type=jnp.float32)
    term_up = jnp.dot(routed.T, grad_up_pre, preferred_element_type=jnp.float32)
    term_down_t = jnp.dot(grad_rows.T, hidden, preferred_element_type=jnp.float32)
    return (row_grad, term_gate, term_up, term_down_t)


def gather_fsdp(shard, n_fsdp):
    copies = jnp.broadcast_to(shard[None], (n_fsdp,) + shard.shape)
    return lax.all_to_all(copies, "fsdp", split_axis=0, concat_axis=0, tiled=True)


def scatter_sum_fsdp(terms, n_fsdp):
    stacked = jnp.stack([t.astype(jnp.bfloat16) for t in terms], axis=0)
    count, rows = (stacked.shape[0], stacked.shape[1] // n_fsdp)
    blocks = stacked.reshape((count, n_fsdp, rows) + stacked.shape[2:]).swapaxes(0, 1)
    got = lax.all_to_all(blocks, "fsdp", split_axis=0, concat_axis=0, tiled=True)
    summed = jnp.sum(got.astype(jnp.float32), axis=0).astype(jnp.bfloat16)
    return [summed[i] for i in range(count)]


def per_device(tokens, expert_ids, route_probs, gate_weight, up_weight, down_weight, cotangent):
    n_expert = lax.axis_size("expert")
    n_fsdp = lax.axis_size("fsdp")
    experts = n_expert * gate_weight.shape[0]
    tok_dev, choose = expert_ids.shape
    features = tokens.shape[1]
    capacity = tok_dev * choose * 9 // (experts * 8)
    slot_count = experts * capacity
    dispatch, counts = routing(expert_ids, experts, capacity)
    dispatch_pair = dispatch.astype(jnp.bfloat16)
    dispatch_tok = jnp.sum(dispatch.reshape(slot_count, tok_dev, choose), axis=2).astype(
        jnp.bfloat16
    )
    outgoing = jnp.dot(dispatch_tok, tokens, preferred_element_type=jnp.float32).astype(
        jnp.bfloat16
    )
    count_rows = jnp.zeros((experts, 1, features), jnp.bfloat16)
    count_rows = count_rows.at[:, 0, 0].set(counts.astype(jnp.bfloat16))
    payload = jnp.concatenate([outgoing.reshape(experts, capacity, features), count_rows], axis=1)
    arrived_all = lax.all_to_all(payload, "expert", split_axis=0, concat_axis=0, tiled=True)
    arrived = arrived_all[:, :capacity]
    arrived_counts = arrived_all[:, capacity, 0:1]
    upstream = cotangent.astype(jnp.float32)
    slot_probs = jnp.sum(jnp.where(dispatch, route_probs.reshape(1, tok_dev * choose), 0.0), axis=1)
    slot_cot = jnp.dot(dispatch_tok, cotangent, preferred_element_type=jnp.float32)
    outgoing_grad = (slot_probs[:, None] * slot_cot).astype(jnp.bfloat16)
    arrived_all, outgoing_grad = lax.optimization_barrier((arrived_all, outgoing_grad))
    arrived_grad = lax.all_to_all(
        outgoing_grad.reshape(experts, capacity, features),
        "expert",
        split_axis=0,
        concat_axis=0,
        tiled=True,
    )
    routed = arrived.reshape(slot_count, features)
    grad_rows = arrived_grad.reshape(slot_count, features)
    live_mask = jnp.arange(capacity, dtype=jnp.float32)[None, :] < arrived_counts.astype(
        jnp.float32
    )
    live_mask = live_mask.astype(jnp.float32).reshape(slot_count)
    w_gate = lax.all_gather(gate_weight, "fsdp", axis=1, tiled=True)[0]
    w_up = lax.all_gather(up_weight, "fsdp", axis=1, tiled=True)[0]
    w_down = lax.all_gather(down_weight, "fsdp", axis=2, tiled=True)[0]
    w_down_blocks = w_down.reshape(w_down.shape[0], n_fsdp, -1).swapaxes(0, 1)
    gate_pre, up_pre, hidden, expert_out = expert_forward(
        routed, live_mask, w_gate, w_up, w_down_blocks
    )
    returned = lax.all_to_all(
        expert_out.reshape(n_expert, capacity, features),
        "expert",
        split_axis=0,
        concat_axis=0,
        tiled=True,
    )
    row_grad, term_gate, term_up, term_down_t = expert_backward(
        routed, grad_rows, gate_pre, up_pre, hidden, w_gate, w_up, w_down_blocks
    )
    returned_grad = lax.all_to_all(
        row_grad.reshape(n_expert, capacity, features),
        "expert",
        split_axis=0,
        concat_axis=0,
        tiled=True,
    )
    summed_gate = lax.psum_scatter(
        term_gate.astype(jnp.bfloat16), "fsdp", scatter_dimension=0, tiled=True
    )
    returned, term_up = lax.optimization_barrier((returned, term_up))
    (summed_up,) = scatter_sum_fsdp([term_up], n_fsdp)
    summed_down = lax.psum_scatter(
        term_down_t.T.astype(jnp.bfloat16), "fsdp", scatter_dimension=1, tiled=True
    )
    combined = lax.dot_general(
        dispatch_pair,
        returned.reshape(slot_count, features),
        (((0,), (0,)), ((), ())),
        preferred_element_type=jnp.float32,
    ).reshape(tok_dev, choose, features)
    mixed = jnp.einsum("tk,tkd->td", route_probs, combined).astype(jnp.bfloat16)
    grad_probs = jnp.einsum("td,tkd->tk", upstream, combined)
    grad_tokens = lax.dot_general(
        dispatch_tok,
        returned_grad.reshape(slot_count, features),
        (((0,), (0,)), ((), ())),
        preferred_element_type=jnp.float32,
    ).astype(jnp.bfloat16)
    return (mixed, grad_probs, grad_tokens, summed_gate[None], summed_up[None], summed_down[None])


def solution(mesh):
    return jax.shard_map(
        per_device,
        mesh=mesh,
        in_specs=(
            P(("expert", "fsdp"), None),
            P(("expert", "fsdp"), None),
            P(("expert", "fsdp"), None),
            P("expert", "fsdp", None),
            P("expert", "fsdp", None),
            P("expert", None, "fsdp"),
            P(("expert", "fsdp"), None),
        ),
        out_specs=(
            P(("expert", "fsdp"), None),
            P(("expert", "fsdp"), None),
            P(("expert", "fsdp"), None),
            P("expert", "fsdp", None),
            P("expert", "fsdp", None),
            P("expert", None, "fsdp"),
        ),
        check_vma=False,
    )
```

profile of v0, /device:TPU:2, one launch (start us, length us, event | category | flops | bytes accessed | tf_op | source)
XLA Modules:
  0.0 421.8 jit_solution(11539978942677578161)
XLA Ops:
  20.3 8.7 %all-to-all-start = ((bf16[16,37,2048]{2,1,0:T(8,128)(2,1)}), bf16[16,37,2048]{2,1,0:T(8,128)(2,1)S(1)}, u32[]{:S(2)}, u32[]{:S(2)}) async-start(bf16[16,37,2048]{2,1,0:T(8,128)(2,1)} %fusion.16), calls=%async_computation | async-start | bytes 5242880 | tf_op jit(solution)/shard_map/all_to_all | solution.py:81
  32.5 57.1 %all-to-all-done = bf16[16,37,2048]{2,1,0:T(8,128)(2,1)S(1)} async-done(((bf16[16,37,2048]{2,1,0:T(8,128)(2,1)}), bf16[16,37,2048]{2,1,0:T(8,128)(2,1)S(1)}, u32[]{:S(2)}, u32[]{:S(2)}) %all-to-all-start) | async-done | bytes 2424864 | tf_op jit(solution)/shard_map/all_to_all | solution.py:81
  89.6 4.5 %reshape.168 = bf16[16,36,2048]{2,1,0:T(8,128)(2,1)} reshape(bf16[576,2048]{1,0:T(8,128)(2,1)} %multiply_convert_fusion) | data formatting | bytes 4718592 | tf_op jit(solution)/shard_map/reshape | solution.py:90
  94.1 4.6 %all-to-all-start.2 = ((bf16[16,36,2048]{2,1,0:T(8,128)(2,1)}), bf16[16,36,2048]{2,1,0:T(8,128)(2,1)S(1)}, u32[]{:S(2)}, u32[]{:S(2)}) async-start(bf16[16,36,2048]{2,1,0:T(8,128)(2,1)} %reshape.168), calls=%async_computation.2 | async-start | bytes 5242880 | tf_op jit(solution)/shard_map/all_to_all | solution.py:89
  103.9 4.4 %copy.83 = bf16[88,8,16,128]{3,2,1,0:T(8,128)(2,1)} copy(bf16[88,8,16,128]{3,1,2,0:T(8,128)(2,1)} %bitcast.86) | data formatting | bytes 5767168
  108.4 17.8 %all-gather.4.cloned.1.call-done = bf16[1,2048,704]{1,2,0:T(8,128)(2,1)} async-done(((bf16[1,128,704]{1,2,0:T(8,128)(2,1)}), bf16[1,2048,704]{1,2,0:T(8,128)(2,1)}) %all-gather.4.cloned.1.call-update) | async-done | bytes 2883600 | tf_op jit(solution)/shard_map/all_gather | solution.py:102
  126.1 5.8 %fusion.14 = f32[576,704]{1,0:T(8,128)} fusion(bf16[576,2048]{1,0:T(8,128)(2,1)} %reshape.167, bf16[1,2048,704]{1,2,0:T(8,128)(2,1)} %all-gather.4.cloned.1.call-done), kind=kOutput, calls=%fused_computation.20 | convolution fusion | flops 1660944384 | bytes 6864896 | tf_op jit(solution)/shard_map/dot_general | solution.py:19
  131.9 27.3 %all-to-all-done.2 = bf16[16,36,2048]{2,1,0:T(8,128)(2,1)S(1)} async-done(((bf16[16,36,2048]{2,1,0:T(8,128)(2,1)}), bf16[16,36,2048]{2,1,0:T(8,128)(2,1)S(1)}, u32[]{:S(2)}, u32[]{:S(2)}) %all-to-all-start.2) | async-done | bytes 2359328 | tf_op jit(solution)/shard_map/all_to_all | solution.py:89
  161.9 5.8 %fusion.5 = f32[576,704,1]{1,0,2:T(8,128)} fusion(bf16[704,16,128]{2,1,0:T(8,128)(2,1)} %bitcast.87, bf16[576,16,128]{2,1,0:T(8,128)(2,1)} %reshape_reshape.7), kind=kOutput, calls=%fused_computation.11 | convolution fusion | flops 1660944384 | bytes 6864896 | tf_op jit(solution)/shard_map/sjd,jfd->sf/dot_general | solution.py:30
  167.7 15.9 %all-gather.6.cloned.1.call-done = bf16[1,2048,704]{1,2,0:T(8,128)(2,1)} async-done(((bf16[1,128,704]{1,2,0:T(8,128)(2,1)}), bf16[1,2048,704]{1,2,0:T(8,128)(2,1)}) %all-gather.6.cloned.1.call-update) | async-done | bytes 2883600 | tf_op jit(solution)/shard_map/all_gather | solution.py:103
  183.6 7.6 %fusion.25 = (bf16[576,704]{1,0:T(8,128)(2,1)}, bf16[576,704]{1,0:T(8,128)(2,1)}, bf16[576,704]{1,0:T(8,128)(2,1)S(1)}) fusion(f32[576,704,1]{1,0,2:T(8,128)} %fusion.5, f32[576,704]{1,0:T(8,128)} %fusion.14, f32[576]{0:T(1024)S(1)} %reshape.174, bf16[576,2048]{1,0:T(8,128)(2,1)} %reshape.167, bf16[1,2048,704]{1,2,0:T(8,128)(2,1)} %all-gather.6.cloned.1.call-done), kind=kOutput, calls=%fused_computation.33 | convolution fusion | flops 1667432448 | bytes 10922240 | tf_op jit(solution)/shard_map/dot_general | solution.py:20
  196.1 4.5 %reshape_reshape.6 = bf16[16,36,2048]{2,1,0:T(8,128)(2,1)} reshape(bf16[576,16,128]{2,1,0:T(8,128)(2,1)} %copy.68) | data formatting | bytes 4718592 | tf_op jit(solution)/shard_map/reshape;reshape | solution.py:110
  200.6 7.2 %all-to-all-start.1 = ((bf16[16,36,2048]{2,1,0:T(8,128)(2,1)}), bf16[16,36,2048]{2,1,0:T(8,128)(2,1)}, u32[]{:S(2)}, u32[]{:S(2)}) async-start(bf16[16,36,2048]{2,1,0:T(8,128)(2,1)} %reshape_reshape.6), calls=%async_computation.1 | async-start | bytes 5242880 | tf_op jit(solution)/shard_map/all_to_all | solution.py:109
  210.2 4.4 %convolution_convert_fusion = bf16[704,2048]{1,0:T(8,128)(2,1)S(1)} fusion(bf16[576,704]{1,0:T(8,128)(2,1)} %copy-done.9, bf16[576,2048]{1,0:T(8,128)(2,1)} %reshape.172), kind=kOutput, calls=%fused_computation.8 | convolution fusion | flops 1662386176 | bytes 6053888 | tf_op jit(solution)/shard_map/dot_general | solution.py:44
  226.7 41.6 %all-to-all-done.1 = bf16[16,36,2048]{2,1,0:T(8,128)(2,1)} async-done(((bf16[16,36,2048]{2,1,0:T(8,128)(2,1)}), bf16[16,36,2048]{2,1,0:T(8,128)(2,1)}, u32[]{:S(2)}, u32[]{:S(2)}) %all-to-all-start.1) | async-done | bytes 2359328 | tf_op jit(solution)/shard_map/all_to_all | solution.py:109
  268.4 4.6 %all-to-all-start.3 = ((bf16[16,36,2048]{2,1,0:T(8,128)(2,1)}), bf16[16,36,2048]{2,1,0:T(8,128)(2,1)S(1)}, u32[]{:S(2)}, u32[]{:S(2)}) async-start(bf16[16,36,2048]{2,1,0:T(8,128)(2,1)} %reshape.170), calls=%async_computation.3 | async-start | bytes 5242880 | tf_op jit(solution)/shard_map/all_to_all | solution.py:119
  273.0 5.9 %convolution_convert_fusion.1 = bf16[2048,704]{0,1:T(8,128)(2,1)} fusion(bf16[576,2048]{1,0:T(8,128)(2,1)} %reshape.167, bf16[576,704]{1,0:T(8,128)(2,1)} %get-tuple-element.26), kind=kOutput, calls=%fused_computation.9 | convolution fusion | flops 1662386176 | bytes 6053888 | tf_op jit(solution)/shard_map/dot_general | solution.py:42
  279.0 4.6 %copy.78 = bf16[2048,704]{1,0:T(8,128)(2,1)} copy(bf16[2048,704]{0,1:T(8,128)(2,1)} %convolution_convert_fusion.1) | data formatting | bytes 5767168
  283.6 4.3 %fusion.39 = bf16[2048,704]{0,1:T(8,128)(2,1)S(1)} fusion(bf16[576,2048]{1,0:T(8,128)(2,1)} %reshape.167, bf16[576,704]{1,0:T(8,128)(2,1)} %get-tuple-element.27), kind=kOutput, calls=%fused_computation.67 | convolution fusion | flops 1660944384 | bytes 6053888 | tf_op jit(solution)/shard_map/dot_general | solution.py:43
  291.2 42.3 %all-to-all-done.3 = bf16[16,36,2048]{2,1,0:T(8,128)(2,1)S(1)} async-done(((bf16[16,36,2048]{2,1,0:T(8,128)(2,1)}), bf16[16,36,2048]{2,1,0:T(8,128)(2,1)S(1)}, u32[]{:S(2)}, u32[]{:S(2)}) %all-to-all-start.3) | async-done | bytes 2359328 | tf_op jit(solution)/shard_map/all_to_all | solution.py:119
  335.0 5.7 %all-to-all-start.4 = ((bf16[16,1,128,704]{2,3,1,0:T(8,128)(2,1)}), bf16[16,1,128,704]{2,3,1,0:T(8,128)(2,1)S(1)}, u32[]{:S(2)}, u32[]{:S(2)}) async-start(bf16[16,1,128,704]{2,3,1,0:T(8,128)(2,1)} %copy.72), calls=%async_computation.4 | async-start | bytes 5767168 | tf_op jit(solution)/shard_map/all_to_all | solution.py:57
  344.0 4.1 reshape.177
  358.0 4.1 reshape.171
  367.1 45.4 %reduce-scatter.7.cloned.1.call-done = bf16[128,704]{1,0:T(8,128)(2,1)} async-done(((bf16[2048,704]{1,0:T(8,128)(2,1)}), bf16[128,704]{1,0:T(8,128)(2,1)}) %reduce-scatter.7.cloned.1.call-update) | async-done | bytes 180240
  (82 shorter events, 69.5 us)
Async XLA Ops:
  7.2 23.1 %copy-start = (bf16[128,2048]{1,0:T(8,128)(2,1)S(1)}, bf16[128,2048]{1,0:T(8,128)(2,1)}, u32[]{:S(2)}) copy-start(bf16[128,2048]{1,0:T(8,128)(2,1)} %param.15) | copy-start | bytes 1572868
  7.2 96.8 %all-gather.8.cloned.1.call-start = ((), (), s32[]{:S(2)}) async-start(), calls=%async_computation.9 | async-start | bytes 3063808 | tf_op jit(solution)/shard_map/all_gather | solution.py:104
  7.9 118.2 %all-gather.4.cloned.1.call-start = ((), (), s32[]{:S(2)}) async-start(), calls=%async_computation.7 | async-start | bytes 3063808 | tf_op jit(solution)/shard_map/all_gather | solution.py:102
  12.4 17.8 %copy-start.3 = (s32[576,128]{1,0:T(8,128)}, s32[576,128]{1,0:T(8,128)S(1)}, u32[]{:S(2)}) copy-start(s32[576,128]{1,0:T(8,128)S(1)} %convert_reduce_fusion) | copy-start | bytes 884740
  20.3 9.5 %copy-start.5 = (f32[128,4]{0,1:T(4,128)S(1)}, f32[128,4]{0,1:T(4,128)}, u32[]{:S(2)}) copy-start(f32[128,4]{0,1:T(4,128)} %param.11) | copy-start | bytes 6148
  20.3 69.2 %all-to-all-start = ((bf16[16,37,2048]{2,1,0:T(8,128)(2,1)}), bf16[16,37,2048]{2,1,0:T(8,128)(2,1)S(1)}, u32[]{:S(2)}, u32[]{:S(2)}) async-start(bf16[16,37,2048]{2,1,0:T(8,128)(2,1)} %fusion.16), calls=%async_computation | async-start | bytes 5242880 | tf_op jit(solution)/shard_map/all_to_all | solution.py:81
  29.0 154.6 %all-gather.6.cloned.1.call-start = ((), (), s32[]{:S(2)}) async-start(), calls=%async_computation.8 | async-start | bytes 3063808 | tf_op jit(solution)/shard_map/all_gather | solution.py:103
  89.6 4.5 %copy-start.1 = (bf16[16,37,2048]{2,1,0:T(8,128)(2,1)}, bf16[16,37,2048]{2,1,0:T(8,128)(2,1)S(1)}, u32[]{:S(2)}) copy-start(bf16[16,37,2048]{2,1,0:T(8,128)(2,1)S(1)} %all-to-all-done) | copy-start | bytes 7274500
  94.1 65.1 %all-to-all-start.2 = ((bf16[16,36,2048]{2,1,0:T(8,128)(2,1)}), bf16[16,36,2048]{2,1,0:T(8,128)(2,1)S(1)}, u32[]{:S(2)}, u32[]{:S(2)}) async-start(bf16[16,36,2048]{2,1,0:T(8,128)(2,1)} %reshape.168), calls=%async_computation.2 | async-start | bytes 5242880 | tf_op jit(solution)/shard_map/all_to_all | solution.py:89
  183.6 7.6 %copy-start.4 = (bf16[88,8,16,128]{3,2,1,0:T(8,128)(2,1)S(1)}, bf16[88,8,16,128]{3,2,1,0:T(8,128)(2,1)}, u32[]{:S(2)}) copy-start(bf16[88,8,16,128]{3,2,1,0:T(8,128)(2,1)} %copy.83) | copy-start | bytes 8650756
  191.1 2.0 copy-start.9
  200.6 67.8 %all-to-all-start.1 = ((bf16[16,36,2048]{2,1,0:T(8,128)(2,1)}), bf16[16,36,2048]{2,1,0:T(8,128)(2,1)}, u32[]{:S(2)}, u32[]{:S(2)}) async-start(bf16[16,36,2048]{2,1,0:T(8,128)(2,1)} %reshape_reshape.6), calls=%async_computation.1 | async-start | bytes 5242880 | tf_op jit(solution)/shard_map/all_to_all | solution.py:109
  207.8 157.6 %reduce-scatter.9.cloned.1.call-start = ((), (), s32[]{:S(2)}) async-start(), calls=%async_computation.11 | async-start | bytes 3342336
  217.3 1.8 copy-start.6
  219.2 3.3 copy-start.7
  219.2 3.3 copy-start.8
  268.4 65.1 %all-to-all-start.3 = ((bf16[16,36,2048]{2,1,0:T(8,128)(2,1)}), bf16[16,36,2048]{2,1,0:T(8,128)(2,1)S(1)}, u32[]{:S(2)}, u32[]{:S(2)}) async-start(bf16[16,36,2048]{2,1,0:T(8,128)(2,1)} %reshape.170), calls=%async_computation.3 | async-start | bytes 5242880 | tf_op jit(solution)/shard_map/all_to_all | solution.py:119
  273.0 139.5 %reduce-scatter.7.cloned.1.call-start = ((), (), s32[]{:S(2)}) async-start(), calls=%async_computation.10 | async-start | bytes 3342336
  333.5 1.5 copy-start.2
  335.0 79.2 %all-to-all-start.4 = ((bf16[16,1,128,704]{2,3,1,0:T(8,128)(2,1)}), bf16[16,1,128,704]{2,3,1,0:T(8,128)(2,1)S(1)}, u32[]{:S(2)}, u32[]{:S(2)}) async-start(bf16[16,1,128,704]{2,3,1,0:T(8,128)(2,1)} %copy.72), calls=%async_computation.4 | async-start | bytes 5767168 | tf_op jit(solution)/shard_map/all_to_all | solution.py:57
Sparse Core Ops, SparseCore 0:
  10.4 58.2 all-gather.7
  71.1 55.0 all-gather.3
  128.5 55.0 all-gather.5
  217.5 81.1 reduce-scatter.8
  302.1 110.2 reduce-scatter.6
where the time goes:
time: 423 us; the launch traced here: 422 us
  waiting for transfers between devices  250 us (59%)
  local copies, waits for them, and re-layouts  61.6 us (15%)
  matrix products  58 us (14%)
  starting transfers between devices  31.2 us (7%)
  between operations  14 us (3%)
  other arithmetic  7.5 us (2%)
    all_to_all x1, waiting for transfers between devices, per_device(): lax.all_to_all(payload, 'expert', split_axis=0, concat_axis=0, tiled=True)  57.1 us
    unnamed x7, waiting for transfers between devices  47.5 us
    all_to_all x1, waiting for transfers between devices, per_device(): lax.all_to_all(row_grad.reshape(n_expert, capacity, features), 'expert',...  42.3 us
    all_to_all x1, waiting for transfers between devices, per_device(): lax.all_to_all(expert_out.reshape(n_expert, capacity, features), 'expert'...  41.6 us
    all_to_all x1, waiting for transfers between devices, per_device(): lax.all_to_all(outgoing_grad.reshape(experts, capacity, features), 'exper...  27.3 us
    unnamed x29, local copies, waits for them, and re-layouts  20.6 us
    all_gather x1, waiting for transfers between devices, per_device(): w_gate = lax.all_gather(gate_weight, 'fsdp', axis=1, tiled=True)[0]  17.8 us
    all_gather x1, waiting for transfers between devices, per_device(): w_up = lax.all_gather(up_weight, 'fsdp', axis=1, tiled=True)[0]  15.9 us
  transfers between devices with their start and end apart: 10, of which 7 were waited for; matrix products, arithmetic and copies ran while one was open for 25% of the time, Pallas kernels for 0%

commit v1 on v0

--- a/solution.py
+++ b/solution.py
@@ -99,7 +99,13 @@
         jnp.float32
     )
     live_mask = live_mask.astype(jnp.float32).reshape(slot_count)
-    w_gate = lax.all_gather(gate_weight, "fsdp", axis=1, tiled=True)[0]
+    unite_the_object = lambda block_here, dev_axis, axis_no: jnp.concatenate(
+        jax.lax.all_to_all(
+            jnp.stack(jax.lax.axis_size(dev_axis) * [block_here], axis=0), dev_axis, 0, 0
+        ),
+        axis=axis_no,
+    )
+    w_gate = unite_the_object(gate_weight, "fsdp", 1)[0]
     w_up = lax.all_gather(up_weight, "fsdp", axis=1, tiled=True)[0]
     w_down = lax.all_gather(down_weight, "fsdp", axis=2, tiled=True)[0]
     w_down_blocks = w_down.reshape(w_down.shape[0], n_fsdp, -1).swapaxes(0, 1)

time: 423 us -> 462 us (1.092); the launches traced: 422 us -> 454 us
  waiting for transfers between devices: 250 us -> 261 us
  local copies, waits for them, and re-layouts: 61.6 us -> 71.9 us
  starting transfers between devices: 31.2 us -> 40.3 us
    all_to_all x0 -> x1, waiting for transfers between devices: none -> 30.6 us  [per_device(): jax.lax.all_to_all(jnp.stack(jax.lax.axis_size(dev_axis) * [block_here],...]
    all_gather x1 -> x0, waiting for transfers between devices: 17.8 us -> none  [per_device(): w_gate = lax.all_gather(gate_weight, 'fsdp', axis=1, tiled=True)[0]]
    all_gather x1, waiting for transfers between devices: 15.9 us -> 0.01 us  [per_device(): w_up = lax.all_gather(up_weight, 'fsdp', axis=1, tiled=True)[0]]
    all_to_all x1, waiting for transfers between devices: 27.3 us -> 39.7 us  [per_device(): lax.all_to_all(outgoing_grad.reshape(experts, capacity, features), 'exper...]
    all_to_all x0 -> x1, starting transfers between devices: none -> 7.61 us  [per_device(): jax.lax.all_to_all(jnp.stack(jax.lax.axis_size(dev_axis) * [block_here],...]
    all_to_all x0 -> x1, local copies, waits for them, and re-layouts: none -> 5.27 us  [per_device(): jax.lax.all_to_all(jnp.stack(jax.lax.axis_size(dev_axis) * [block_here],...]
    unnamed x29 -> x33, local copies, waits for them, and re-layouts: 20.6 us -> 23.2 us
    unnamed x7 -> x6, waiting for transfers between devices: 47.5 us -> 47.6 us
  transfers between devices with their start and end apart: 10 -> 10, of which waited for: 7 -> 6; matrix products, arithmetic and copies ran while one was open for 25% -> 23% of each run, Pallas kernels for 0% -> 0%
where the time goes in v1:
time: 462 us; the launch traced here: 454 us
  waiting for transfers between devices  261 us (56%)
  local copies, waits for them, and re-layouts  71.9 us (16%)
  matrix products  58.9 us (13%)
  starting transfers between devices  40.3 us (9%)
  between operations  14.2 us (3%)
  other arithmetic  7.38 us (2%)
    all_to_all x1, waiting for transfers between devices, per_device(): lax.all_to_all(payload, 'expert', split_axis=0, concat_axis=0, tiled=True)  59.8 us
    unnamed x6, waiting for transfers between devices  47.6 us
    all_to_all x1, waiting for transfers between devices, per_device(): lax.all_to_all(row_grad.reshape(n_expert, capacity, features), 'expert',...  42.1 us
    all_to_all x1, waiting for transfers between devices, per_device(): lax.all_to_all(expert_out.reshape(n_expert, capacity, features), 'expert'...  41.7 us
    all_to_all x1, waiting for transfers between devices, per_device(): lax.all_to_all(outgoing_grad.reshape(experts, capacity, features), 'exper...  39.7 us
    all_to_all x1, waiting for transfers between devices, per_device(): jax.lax.all_to_all(jnp.stack(jax.lax.axis_size(dev_axis) * [block_here],...  30.6 us
    unnamed x33, local copies, waits for them, and re-layouts  23.2 us
  transfers between devices with their start and end apart: 10, of which 6 were waited for; matrix products, arithmetic and copies ran while one was open for 23% of the time, Pallas kernels for 0%

profile of v1, /device:TPU:2, one launch (start us, length us, event | category | flops | bytes accessed | tf_op | source)
XLA Modules:
  0.0 454.2 jit_solution(8451166815954876035)
XLA Ops:
  19.4 8.7 %all-to-all-start = ((bf16[16,37,2048]{2,1,0:T(8,128)(2,1)}), bf16[16,37,2048]{2,1,0:T(8,128)(2,1)S(1)}, u32[]{:S(2)}, u32[]{:S(2)}) async-start(bf16[16,37,2048]{2,1,0:T(8,128)(2,1)} %fusion.16), calls=%async_computation | async-start | bytes 5242880 | tf_op jit(solution)/shard_map/all_to_all | solution.py:81
  28.8 59.8 %all-to-all-done = bf16[16,37,2048]{2,1,0:T(8,128)(2,1)S(1)} async-done(((bf16[16,37,2048]{2,1,0:T(8,128)(2,1)}), bf16[16,37,2048]{2,1,0:T(8,128)(2,1)S(1)}, u32[]{:S(2)}, u32[]{:S(2)}) %all-to-all-start) | async-done | bytes 2424864 | tf_op jit(solution)/shard_map/all_to_all | solution.py:81
  91.0 7.6 %all-to-all-start.1 = ((bf16[16,1,128,704]{2,3,1,0:T(8,128)(2,1)}), bf16[16,1,128,704]{2,3,1,0:T(8,128)(2,1)S(1)}, u32[]{:S(2)}, u32[]{:S(2)}) async-start(bf16[16,1,128,704]{2,3,1,0:T(8,128)(2,1)} %stack.2), calls=%async_computation.1 | async-start | bytes 5767168 | tf_op jit(solution)/shard_map/all_to_all | solution.py:103
  107.0 30.6 %all-to-all-done.1 = bf16[16,1,128,704]{2,3,1,0:T(8,128)(2,1)S(1)} async-done(((bf16[16,1,128,704]{2,3,1,0:T(8,128)(2,1)}), bf16[16,1,128,704]{2,3,1,0:T(8,128)(2,1)S(1)}, u32[]{:S(2)}, u32[]{:S(2)}) %all-to-all-start.1) | async-done | bytes 2883616 | tf_op jit(solution)/shard_map/all_to_all | solution.py:103
  139.2 6.9 %all-to-all-start.3 = ((bf16[16,36,2048]{2,1,0:T(8,128)(2,1)}), bf16[16,36,2048]{2,1,0:T(8,128)(2,1)S(1)}, u32[]{:S(2)}, u32[]{:S(2)}) async-start(bf16[16,36,2048]{2,1,0:T(8,128)(2,1)} %reshape.171), calls=%async_computation.3 | async-start | bytes 5242880 | tf_op jit(solution)/shard_map/all_to_all | solution.py:89
  146.1 5.3 %copy.84 = bf16[16,1,128,704]{2,0,3,1:T(8,128)(2,1)} copy(bf16[16,1,128,704]{2,3,1,0:T(8,128)(2,1)} %copy-done.1) | data formatting | bytes 5767168 | tf_op jit(solution)/shard_map/all_to_all | solution.py:103
  156.6 5.9 %fusion.7 = f32[576,704]{1,0:T(8,128)} fusion(bf16[576,2048]{1,0:T(8,128)(2,1)} %reshape.170, bf16[88,8,16,128]{3,2,1,0:T(8,128)(2,1)} %bitcast.91), kind=kOutput, calls=%fused_computation.13 | convolution fusion | flops 1660944384 | bytes 6864896 | tf_op jit(solution)/shard_map/dot_general | solution.py:19
  162.5 4.4 copy.102
  166.9 39.7 %all-to-all-done.3 = bf16[16,36,2048]{2,1,0:T(8,128)(2,1)S(1)} async-done(((bf16[16,36,2048]{2,1,0:T(8,128)(2,1)}), bf16[16,36,2048]{2,1,0:T(8,128)(2,1)S(1)}, u32[]{:S(2)}, u32[]{:S(2)}) %all-to-all-start.3) | async-done | bytes 2359328 | tf_op jit(solution)/shard_map/all_to_all | solution.py:89
  209.7 5.8 %fusion.9 = f32[576,704,1]{1,0,2:T(8,128)} fusion(bf16[704,16,128]{2,1,0:T(8,128)(2,1)} %bitcast.94, bf16[576,16,128]{2,1,0:T(8,128)(2,1)} %reshape_reshape.7), kind=kOutput, calls=%fused_computation.15 | convolution fusion | flops 1660944384 | bytes 6864896 | tf_op jit(solution)/shard_map/sjd,jfd->sf/dot_general | solution.py:30
  215.5 7.6 %fusion.27 = (bf16[576,704]{1,0:T(8,128)(2,1)}, bf16[576,704]{1,0:T(8,128)(2,1)}, bf16[576,704]{1,0:T(8,128)(2,1)S(1)}) fusion(f32[576,704,1]{1,0,2:T(8,128)} %fusion.9, f32[576,704]{1,0:T(8,128)} %fusion.7, f32[576]{0:T(1024)S(1)} %reshape.177, bf16[576,2048]{1,0:T(8,128)(2,1)} %reshape.170, bf16[1,2048,704]{1,2,0:T(8,128)(2,1)} %all-gather.3.cloned.1.call-done), kind=kOutput, calls=%fused_computation.35 | convolution fusion | flops 1667432448 | bytes 10922240 | tf_op jit(solution)/shard_map/dot_general | solution.py:20
  228.0 4.5 reshape_reshape.6
  232.5 4.6 %all-to-all-start.2 = ((bf16[16,36,2048]{2,1,0:T(8,128)(2,1)}), bf16[16,36,2048]{2,1,0:T(8,128)(2,1)}, u32[]{:S(2)}, u32[]{:S(2)}) async-start(bf16[16,36,2048]{2,1,0:T(8,128)(2,1)} %reshape_reshape.6), calls=%async_computation.2 | async-start | bytes 5242880 | tf_op jit(solution)/shard_map/all_to_all | solution.py:115
  239.5 4.4 convolution_convert_fusion
  256.1 41.7 %all-to-all-done.2 = bf16[16,36,2048]{2,1,0:T(8,128)(2,1)} async-done(((bf16[16,36,2048]{2,1,0:T(8,128)(2,1)}), bf16[16,36,2048]{2,1,0:T(8,128)(2,1)}, u32[]{:S(2)}, u32[]{:S(2)}) %all-to-all-start.2) | async-done | bytes 2359328 | tf_op jit(solution)/shard_map/all_to_all | solution.py:115
  297.8 4.6 %all-to-all-start.4 = ((bf16[16,36,2048]{2,1,0:T(8,128)(2,1)}), bf16[16,36,2048]{2,1,0:T(8,128)(2,1)S(1)}, u32[]{:S(2)}, u32[]{:S(2)}) async-start(bf16[16,36,2048]{2,1,0:T(8,128)(2,1)} %reshape.173), calls=%async_computation.4 | async-start | bytes 5242880 | tf_op jit(solution)/shard_map/all_to_all | solution.py:125
  302.4 5.9 %convolution_convert_fusion.1 = bf16[2048,704]{0,1:T(8,128)(2,1)} fusion(bf16[576,2048]{1,0:T(8,128)(2,1)} %reshape.170, bf16[576,704]{1,0:T(8,128)(2,1)} %get-tuple-element.26), kind=kOutput, calls=%fused_computation.9 | convolution fusion | flops 1662386176 | bytes 6053888 | tf_op jit(solution)/shard_map/dot_general | solution.py:42
  308.3 4.8 %copy.96 = bf16[2048,704]{1,0:T(8,128)(2,1)} copy(bf16[2048,704]{0,1:T(8,128)(2,1)} %convolution_convert_fusion.1) | data formatting | bytes 5767168
  313.2 4.4 fusion.41
  320.8 42.1 %all-to-all-done.4 = bf16[16,36,2048]{2,1,0:T(8,128)(2,1)S(1)} async-done(((bf16[16,36,2048]{2,1,0:T(8,128)(2,1)}), bf16[16,36,2048]{2,1,0:T(8,128)(2,1)S(1)}, u32[]{:S(2)}, u32[]{:S(2)}) %all-to-all-start.4) | async-done | bytes 2359328 | tf_op jit(solution)/shard_map/all_to_all | solution.py:125
  364.4 7.7 %all-to-all-start.5 = ((bf16[16,1,128,704]{2,3,1,0:T(8,128)(2,1)}), bf16[16,1,128,704]{2,3,1,0:T(8,128)(2,1)S(1)}, u32[]{:S(2)}, u32[]{:S(2)}) async-start(bf16[16,1,128,704]{2,3,1,0:T(8,128)(2,1)} %copy.90), calls=%async_computation.5 | async-start | bytes 5767168 | tf_op jit(solution)/shard_map/all_to_all | solution.py:57
  375.4 4.2 reshape.180
  389.4 4.1 reshape.174
  398.5 46.2 %reduce-scatter.7.cloned.1.call-done = bf16[128,704]{1,0:T(8,128)(2,1)} async-done(((bf16[2048,704]{1,0:T(8,128)(2,1)}), bf16[128,704]{1,0:T(8,128)(2,1)}) %reduce-scatter.7.cloned.1.call-update) | async-done | bytes 180240
  (87 shorter events, 78.7 us)
Async XLA Ops:
  7.2 92.6 %copy-start = (bf16[128,2048]{1,0:T(8,128)(2,1)S(1)}, bf16[128,2048]{1,0:T(8,128)(2,1)}, u32[]{:S(2)}) copy-start(bf16[128,2048]{1,0:T(8,128)(2,1)} %param.15) | copy-start | bytes 1572868
  10.9 0.7 copy-start.4
  19.4 69.2 %copy-start.7 = (bf16[1,128,704]{1,2,0:T(8,128)(2,1)S(1)}, bf16[1,128,704]{1,2,0:T(8,128)(2,1)}, u32[]{:S(2)}) copy-start(bf16[1,128,704]{1,2,0:T(8,128)(2,1)} %param.12) | copy-start | bytes 540676
  19.4 69.2 %all-to-all-start = ((bf16[16,37,2048]{2,1,0:T(8,128)(2,1)}), bf16[16,37,2048]{2,1,0:T(8,128)(2,1)S(1)}, u32[]{:S(2)}, u32[]{:S(2)}) async-start(bf16[16,37,2048]{2,1,0:T(8,128)(2,1)} %fusion.16), calls=%async_computation | async-start | bytes 5242880 | tf_op jit(solution)/shard_map/all_to_all | solution.py:81
  28.1 134.4 %all-gather.5.cloned.1.call-start = ((), (), s32[]{:S(2)}) async-start(), calls=%async_computation.9 | async-start | bytes 3063808 | tf_op jit(solution)/shard_map/all_gather | solution.py:110
  88.6 2.4 copy-start.2
  91.0 8.4 %copy-start.8 = (f32[128,4]{0,1:T(4,128)S(1)}, f32[128,4]{0,1:T(4,128)}, u32[]{:S(2)}) copy-start(f32[128,4]{0,1:T(4,128)} %param.11) | copy-start | bytes 6148
  91.0 46.7 %all-to-all-start.1 = ((bf16[16,1,128,704]{2,3,1,0:T(8,128)(2,1)}), bf16[16,1,128,704]{2,3,1,0:T(8,128)(2,1)S(1)}, u32[]{:S(2)}, u32[]{:S(2)}) async-start(bf16[16,1,128,704]{2,3,1,0:T(8,128)(2,1)} %stack.2), calls=%async_computation.1 | async-start | bytes 5767168 | tf_op jit(solution)/shard_map/all_to_all | solution.py:103
  98.6 116.9 %all-gather.3.cloned.1.call-start = ((), (), s32[]{:S(2)}) async-start(), calls=%async_computation.8 | async-start | bytes 3063808 | tf_op jit(solution)/shard_map/all_gather | solution.py:109
  137.6 1.6 copy-start.1
  139.2 67.4 %all-to-all-start.3 = ((bf16[16,36,2048]{2,1,0:T(8,128)(2,1)}), bf16[16,36,2048]{2,1,0:T(8,128)(2,1)S(1)}, u32[]{:S(2)}, u32[]{:S(2)}) async-start(bf16[16,36,2048]{2,1,0:T(8,128)(2,1)} %reshape.171), calls=%async_computation.3 | async-start | bytes 5242880 | tf_op jit(solution)/shard_map/all_to_all | solution.py:89
  215.5 7.6 %copy-start.6 = (bf16[88,8,16,128]{3,2,1,0:T(8,128)(2,1)S(1)}, bf16[88,8,16,128]{3,2,1,0:T(8,128)(2,1)}, u32[]{:S(2)}) copy-start(bf16[88,8,16,128]{3,2,1,0:T(8,128)(2,1)} %copy.102) | copy-start | bytes 8650756
  223.1 2.0 copy-start.11
  232.5 65.2 %all-to-all-start.2 = ((bf16[16,36,2048]{2,1,0:T(8,128)(2,1)}), bf16[16,36,2048]{2,1,0:T(8,128)(2,1)}, u32[]{:S(2)}, u32[]{:S(2)}) async-start(bf16[16,36,2048]{2,1,0:T(8,128)(2,1)} %reshape_reshape.6), calls=%async_computation.2 | async-start | bytes 5242880 | tf_op jit(solution)/shard_map/all_to_all | solution.py:115
  237.2 159.6 %reduce-scatter.9.cloned.1.call-start = ((), (), s32[]{:S(2)}) async-start(), calls=%async_computation.11 | async-start | bytes 3342336
  246.7 1.8 copy-start.5
  248.5 3.3 copy-start.9
  248.5 3.3 copy-start.10
  297.8 65.1 %all-to-all-start.4 = ((bf16[16,36,2048]{2,1,0:T(8,128)(2,1)}), bf16[16,36,2048]{2,1,0:T(8,128)(2,1)S(1)}, u32[]{:S(2)}, u32[]{:S(2)}) async-start(bf16[16,36,2048]{2,1,0:T(8,128)(2,1)} %reshape.173), calls=%async_computation.4 | async-start | bytes 5242880 | tf_op jit(solution)/shard_map/all_to_all | solution.py:125
  302.4 142.3 %reduce-scatter.7.cloned.1.call-start = ((), (), s32[]{:S(2)}) async-start(), calls=%async_computation.10 | async-start | bytes 3342336
  362.9 1.5 copy-start.3
  364.4 81.9 %all-to-all-start.5 = ((bf16[16,1,128,704]{2,3,1,0:T(8,128)(2,1)}), bf16[16,1,128,704]{2,3,1,0:T(8,128)(2,1)S(1)}, u32[]{:S(2)}, u32[]{:S(2)}) async-start(bf16[16,1,128,704]{2,3,1,0:T(8,128)(2,1)} %copy.90), calls=%async_computation.5 | async-start | bytes 5767168 | tf_op jit(solution)/shard_map/all_to_all | solution.py:57
Sparse Core Ops, SparseCore 0:
  31.3 56.8 all-gather.4
  101.8 67.9 all-gather.2
  246.9 83.0 reduce-scatter.8
  333.4 111.1 reduce-scatter.6
